TPU v7x, 256 devices: a whole 4x4x8 slice. The times are simulated.
256 devices in a mesh: dp: 64 (over y, z, core), seq: 4 (over x).
Axes of the slice: x: 4, y: 4, z: 8, core: 2. Of those that a mesh axis runs over, the one named last changes fastest.
Arguments:
- frames: bfloat16 [32768, 1536], P('dp', 'seq')
- owner_slot: int32 [32768], P('dp'), may hold values from -1 to 32767, as said below
- segment: int32 [64, 512], P('dp'), may hold values from 0 to 2, never falling along the last dimension, each value on 1 to 256 neighbouring positions
- norm_gain: float32 [1536], replicated, may hold values from 0.25 to 1.75
- expand: bfloat16 [1536, 2, 1536], P('dp', None, 'seq'), may hold values from -0.15625 to 0.15625
- kernel: float32 [9, 1536], P(None, 'seq'), may hold values from -2.5 to 2.5
- project: bfloat16 [1536, 1536], P('seq', 'dp'), may hold values from -0.15625 to 0.15625
- cotangent: bfloat16 [32768, 1536], P('dp', 'seq'), may hold values from -6 to 6
Outputs:
- output: bfloat16 [32768, 1536], P('dp', 'seq')
- grad_frames: bfloat16 [32768, 1536], P('dp', 'seq')
- grad_gain: float32 [1536], P('seq')
- grad_kernel: float32 [9, 1536], P(None, 'seq')
- grad_expand: float32 [1536, 2, 1536], P('dp', None, 'seq')
- grad_project: float32 [1536, 1536], P('seq', 'dp')
Inputs may be any that keep to these rules, and one draw needn't show every extreme that they name: `owner_slot`: for each arrival row, the balanced row that takes it, or -1 for an empty arrival row; no balanced row is named twice. The live rows of each pack come first, contiguous, ordered by sending index of dp and then by arrival row; empty rows fill the pack's tail. Of the 512 arrival rows of one index of dp, at most 8 name rows of any one pack; some pack takes exactly 8 rows from every index of dp. `segment`: within each pack the utterance numbers never fall; a pack holds 3 utterances of 1 to 256 frames, one of exactly 256.
All inputs are finite; a program needn't handle non-finite values.
Results may differ from a plain program's by a relative error of at most 0.01.
Values may be sent and summed in bfloat16 or wider, within the bound.
No kernel may reach another device: no remote copies, remote signals or barrier semaphores. Data moves between devices by JAX's collectives and lax.ppermute only.
A program may use at most 128 MiB of HBM per device.

v0:
```python
import math

import jax
import jax.numpy as jnp
from jax import lax
from jax.sharding import PartitionSpec as P

D = 1536
KSIZE = 9


EPS = 1e-05


def conv_masks(labels):
    half_width = (KSIZE - 1) // 2
    length = labels.shape[0]
    padded = jnp.pad(labels, (half_width, half_width), constant_values=-1)
    return [
        (padded[tap_index : tap_index + length] == labels).astype(jnp.float32)[:, None]
        for tap_index in range(KSIZE)
    ]


def depthwise(signal, kernel, tap_masks):
    half_width = (KSIZE - 1) // 2
    length = signal.shape[0]
    padded = jnp.pad(signal, ((half_width, half_width), (0, 0)))
    total = jnp.zeros(signal.shape, jnp.float32)
    for tap_index in range(KSIZE):
        total = (
            total
            + kernel[tap_index] * padded[tap_index : tap_index + length] * tap_masks[tap_index]
        )
    return total


def depthwise_back(signal, upstream, kernel, tap_masks):
    half_width = (KSIZE - 1) // 2
    length = signal.shape[0]
    padded = jnp.pad(signal, ((half_width, half_width), (0, 0)))
    spread = jnp.zeros((length + 2 * half_width, signal.shape[1]), jnp.float32)
    tap_sums = []
    for tap_index in range(KSIZE):
        masked = upstream * tap_masks[tap_index]
        tap_sums.append(jnp.sum(masked * padded[tap_index : tap_index + length], axis=0))
        spread = spread + jnp.pad(
            kernel[tap_index] * masked, ((tap_index, 2 * half_width - tap_index), (0, 0))
        )
    return (jnp.stack(tap_sums), spread[half_width : half_width + length])


def place_rows(incoming, landing, row_count):
    flat = incoming.reshape(-1, incoming.shape[-1])
    total_slots = flat.shape[0]
    inverse = (
        jnp.full((row_count + 1,), total_slots, jnp.int32)
        .at[landing.reshape(-1)]
        .set(jnp.arange(total_slots, dtype=jnp.int32))[:row_count]
    )
    padded = jnp.concatenate([flat, jnp.zeros((1, flat.shape[1]), flat.dtype)])
    return (padded[inverse], inverse < total_slots)


def shards(frames, owner_slot, segment, norm_gain, expand, kernel, project, cotangent):
    row_count, quarter = frames.shape
    groups = lax.axis_size("dp")
    lane_index = lax.axis_index("seq")
    capacity = row_count // groups
    bucket_slots = groups * capacity
    dest_group = jnp.where(owner_slot >= 0, owner_slot // row_count, groups)
    onehot = (dest_group[:, None] == jnp.arange(groups, dtype=jnp.int32)[None, :]).astype(jnp.int32)
    earlier = jnp.cumsum(onehot, axis=0) - onehot
    within = jnp.sum(earlier * onehot, axis=1)
    send_pos = jnp.where(owner_slot >= 0, dest_group * capacity + within, bucket_slots)
    source_row = (
        jnp.full((bucket_slots + 1,), row_count, jnp.int32)
        .at[send_pos]
        .set(jnp.arange(row_count, dtype=jnp.int32))[:bucket_slots]
    )
    slot_padded = jnp.concatenate([owner_slot, jnp.full((1,), -1, jnp.int32)])
    named_slot = slot_padded[source_row]
    landing_out = jnp.where(named_slot >= 0, named_slot % row_count, row_count).reshape(
        groups, capacity
    )
    padded_in = jnp.concatenate([frames, jnp.zeros((1, quarter), jnp.bfloat16)])
    outgoing = padded_in[source_row].reshape(groups, capacity, quarter)
    incoming, landing = (
        lax.all_to_all(outgoing, "dp", split_axis=0, concat_axis=0, tiled=True),
        lax.all_to_all(landing_out, "dp", split_axis=0, concat_axis=0, tiled=True),
    )
    local_rows, occupied = place_rows(incoming, landing, row_count)
    whole_rows = lax.all_gather(local_rows, "seq", axis=1, tiled=True)
    live_col = occupied.astype(jnp.float32)[:, None]
    floats = whole_rows.astype(jnp.float32)
    row_mean = jnp.mean(floats, axis=1, keepdims=True)
    centred = floats - row_mean
    inv_scale = lax.rsqrt(jnp.mean(centred * centred, axis=1, keepdims=True) + EPS)
    normed = centred * inv_scale
    scaled = (normed * norm_gain).astype(jnp.bfloat16)
    expand_full = lax.all_gather(expand, "dp", axis=0, tiled=True).reshape(D, 2 * quarter)
    project_full = lax.all_gather(project, "dp", axis=1, tiled=True)
    joined = jnp.dot(scaled, expand_full, preferred_element_type=jnp.float32)
    value_half = joined[:, :quarter]
    gate_sig = jax.nn.sigmoid(joined[:, quarter:])
    glu_out = value_half * gate_sig
    tap_masks = conv_masks(segment[0])
    conv_out = depthwise(glu_out, kernel, tap_masks)
    conv_sig = jax.nn.sigmoid(conv_out)
    hidden = (conv_out * conv_sig * live_col).astype(jnp.bfloat16)
    partial_out = jnp.dot(hidden, project_full, preferred_element_type=jnp.float32)
    mixed_share = lax.psum_scatter(
        partial_out.astype(jnp.bfloat16), "seq", scatter_dimension=1, tiled=True
    ).astype(jnp.float32)
    output = (local_rows.astype(jnp.float32) + mixed_share).astype(jnp.bfloat16)
    inv_root = 1.0 / math.sqrt(row_count * groups)
    cot_full = lax.all_gather(cotangent, "seq", axis=1, tiled=True)
    project_term = lax.dot_general(
        hidden, cot_full, (((0,), (0,)), ((), ())), preferred_element_type=jnp.float32
    )
    grad_project = lax.psum_scatter(project_term, "dp", scatter_dimension=1, tiled=True) * inv_root
    hidden_grad = (
        lax.dot_general(
            cot_full, project_full, (((1,), (1,)), ((), ())), preferred_element_type=jnp.float32
        )
        * live_col
    )
    conv_grad = hidden_grad * (conv_sig + conv_out * conv_sig * (1.0 - conv_sig))
    kernel_term, glu_grad = depthwise_back(glu_out, conv_grad, kernel, tap_masks)
    proj_grad = jnp.concatenate(
        [glu_grad * gate_sig, glu_grad * value_half * gate_sig * (1.0 - gate_sig)], axis=1
    ).astype(jnp.bfloat16)
    term_block = lax.dot_general(
        scaled, proj_grad, (((0,), (0,)), ((), ())), preferred_element_type=jnp.float32
    )
    grad_expand = (
        lax.psum_scatter(
            term_block.reshape(expand.shape[0] * lax.axis_size("dp"), 2, quarter),
            "dp",
            scatter_dimension=0,
            tiled=True,
        )
        * inv_root
    )
    scaled_part = lax.dot_general(
        proj_grad, expand_full, (((1,), (1,)), ((), ())), preferred_element_type=jnp.float32
    )
    normed_local = lax.dynamic_slice_in_dim(normed, lane_index * quarter, quarter, 1)
    scaled_grad = lax.psum(scaled_part.astype(jnp.bfloat16), "seq").astype(jnp.float32)
    normed_grad = scaled_grad * norm_gain
    first_mean = jnp.mean(normed_grad, axis=1, keepdims=True)
    second_mean = jnp.mean(normed_grad * normed, axis=1, keepdims=True)
    full_grad = inv_scale * (normed_grad - first_mean - normed * second_mean)
    packed_grad = lax.dynamic_slice_in_dim(full_grad, lane_index * quarter, quarter, 1)
    scaled_share = lax.dynamic_slice_in_dim(scaled_grad, lane_index * quarter, quarter, 1)
    gain_term = jnp.sum(scaled_share * normed_local, axis=0)
    gain_sum, kernel_sum = lax.psum((gain_term, kernel_term), "dp")
    back_rows = (packed_grad + cotangent.astype(jnp.float32)).astype(jnp.bfloat16)
    back_padded = jnp.concatenate([back_rows, jnp.zeros((1, quarter), jnp.bfloat16)])
    returning = back_padded[landing.reshape(-1)].reshape(groups, capacity, quarter)
    returned = lax.all_to_all(returning, "dp", split_axis=0, concat_axis=0, tiled=True)
    returned_flat = jnp.concatenate(
        [returned.reshape(bucket_slots, quarter), jnp.zeros((1, quarter), jnp.bfloat16)]
    )
    grad_frames = returned_flat[send_pos]
    return (
        output,
        grad_frames,
        gain_sum * inv_root,
        kernel_sum * inv_root,
        grad_expand,
        grad_project,
    )


def solution(mesh):
    placed = (
        P("dp", "seq"),
        P("dp"),
        P("dp", None),
        P(),
        P("dp", None, "seq"),
        P(None, "seq"),
        P("seq", "dp"),
        P("dp", "seq"),
    )
    return jax.shard_map(
        shards,
        mesh=mesh,
        in_specs=placed,
        out_specs=(
            P("dp", "seq"),
            P("dp", "seq"),
            P("seq"),
            P(None, "seq"),
            P("dp", None, "seq"),
            P("seq", "dp"),
        ),
        check_vma=False,
    )
```

profile of v0, /device:TPU:4, one launch (start us, length us, event | category | flops | bytes accessed | tf_op | source)
XLA Modules:
  0.0 722.8 jit_solution(6718990988851698500)
XLA Ops:
  7.2 0.7 fusion.22
  7.9 0.7 fusion.55
  8.6 1.2 reduce-window.6
  10.2 0.7 compare_select_fusion.3
  10.9 2.4 scatter_custom_fusion
  13.4 0.7 pad_add_fusion.7
  14.1 2.3 gather_fusion.1
  17.1 12.1 %all-to-all-start.1 = ((s32[64,1,8]{2,1,0:T(1,128)}), s32[64,1,8]{2,1,0:T(1,128)S(1)}, u32[]{:S(2)}, u32[]{:S(2)}) async-start(s32[64,1,8]{2,1,0:T(1,128)} %bitcast.4), calls=%async_computation.1 | async-start | bytes 65536 | tf_op jit(solution)/shard_map/all_to_all | solution.py:90
  29.3 2.6 gather_fusion
  31.9 6.8 all-to-all-done.1
  38.7 4.6 all-to-all-start
  43.9 0.7 reduce.23
  44.8 2.4 scatter_custom_fusion.1
  47.2 10.6 %all-to-all-done = bf16[64,8,384]{2,1,0:T(8,128)(2,1)S(1)} async-done(((bf16[64,8,384]{2,1,0:T(8,128)(2,1)}), bf16[64,8,384]{2,1,0:T(8,128)(2,1)S(1)}, u32[]{:S(2)}, u32[]{:S(2)}) %all-to-all-start) | async-done | bytes 393248 | tf_op jit(solution)/shard_map/all_to_all | solution.py:89
  57.9 2.6 gather_fusion.2
  60.6 0.7 all-gather.6.cloned.1.call-update
  61.3 0.7 all-gather.8.cloned.1.call-update
  63.0 22.6 %all-gather.12.cloned.1.call-done = bf16[512,1536]{1,0:T(8,128)(2,1)} async-done(((bf16[512,384]{1,0:T(8,128)(2,1)}), bf16[512,1536]{1,0:T(8,128)(2,1)}) %all-gather.12.cloned.1.call-update) | async-done | bytes 1572880 | tf_op jit(solution)/shard_map/all_gather | solution.py:93
  85.6 1.8 convert_reduce_fusion
  88.0 79.3 %all-gather.6.cloned.1.call-done = bf16[1536,2,384]{2,1,0:T(2,128)(2,1)} async-done(((bf16[24,2,384]{2,1,0:T(2,128)(2,1)}), bf16[1536,2,384]{2,1,0:T(2,128)(2,1)}) %all-gather.6.cloned.1.call-update) | async-done | bytes 2359312 | tf_op jit(solution)/shard_map/all_gather | solution.py:101
  167.3 2.1 copy.23
  169.5 1.5 fusion.13
  171.2 0.9 copy-done.3
  172.1 2.0 multiply_add_fusion
  174.1 70.2 %all-gather.8.cloned.1.call-done = bf16[384,1536]{0,1:T(8,128)(2,1)} async-done(((bf16[384,24]{0,1:T(8,128)(2,1)}), bf16[384,1536]{0,1:T(8,128)(2,1)}) %all-gather.8.cloned.1.call-update) | async-done | bytes 1179664 | tf_op jit(solution)/shard_map/all_gather | solution.py:102
  244.4 27.2 %all-gather.10.cloned.1.call-done = bf16[512,1536]{1,0:T(8,128)(2,1)} async-done(((bf16[512,384]{1,0:T(8,128)(2,1)}), bf16[512,1536]{1,0:T(8,128)(2,1)}) %all-gather.10.cloned.1.call-update) | async-done | bytes 1572880 | tf_op jit(solution)/shard_map/all_gather | solution.py:117
  271.6 7.9 %multiply_reduce_fusion.1 = (f32[384]{0:T(512)}, f32[384]{0:T(512)}, f32[384]{0:T(512)}, f32[384]{0:T(512)}, f32[384]{0:T(512)}, /*index=5*/f32[384]{0:T(512)}, ...) fusion(f32[512,384]{1,0:T(8,128)} %copy-done.3, ...), kind=kOutput, calls=%fused_computation.36 | convolution fusion | flops 611054208 | bytes 5932032 | tf_op jit(solution)/shard_map/dot_general | solution.py:123
  279.5 0.7 multiply_multiply_fusion.7
  281.3 0.7 copy-done.8
  282.0 0.8 copy-done.5
  282.8 2.6 convolution_convert_fusion
  285.5 4.8 fusion.12
  290.3 8.2 %copy.19 = f32[1536,2,384]{2,1,0:T(2,128)} copy(f32[1536,2,384]{0,2,1:T(8,128)} %bitcast.41) | data formatting | bytes 9437184 | tf_op jit(solution)/shard_map/reshape | solution.py:138
  299.1 2.6 convolution_convert_fusion.1
  301.7 1.6 copy.20
  303.5 4.2 fusion.46
  308.4 32.9 %all-reduce.21.cloned.1.call-done = bf16[512,1536]{1,0:T(8,128)(2,1)} async-done(((bf16[512,1536]{1,0:T(8,128)(2,1)}), bf16[512,1536]{1,0:T(8,128)(2,1)}) %all-reduce.21.cloned.1.call-update) | async-done | bytes 1572880 | tf_op jit(solution)/shard_map/psum | solution.py:149
  341.3 1.9 convert_element_type.110
  343.2 1.1 fusion.11
  344.8 2.6 gather_fusion.3
  347.4 10.5 %all-to-all-start.2 = ((bf16[64,8,384]{2,1,0:T(8,128)(2,1)}), bf16[64,8,384]{2,1,0:T(8,128)(2,1)S(1)}, u32[]{:S(2)}, u32[]{:S(2)}) async-start(bf16[64,8,384]{2,1,0:T(8,128)(2,1)} %bitcast.7), calls=%async_computation.2 | async-start | bytes 786432 | tf_op jit(solution)/shard_map/all_to_all | solution.py:161
  359.4 251.8 %all-reduce.17 = (f32[384]{0:T(512)S(1)}, f32[9,384]{1,0:T(8,128)S(1)}) all-reduce(f32[384]{0:T(512)S(1)} %get-tuple-element.30, f32[9,384]{1,0:T(8,128)S(1)} %stack.39), channel_id=1, replica_groups=mesh['dp'=64,'seq'=4] {'dp'}, use_global_device_ids=true, to_apply=%region_12.13 | all-reduce | flops 3840 | bytes 30720 | tf_op jit(solution)/shard_map/psum | solution.py:157
  612.4 2.6 gather_fusion.4
  615.0 1.6 dynamic-slice_multiply_fusion
  616.6 1.2 copy.21
  617.8 0.8 add_convert_fusion
  618.6 95.9 %reduce-scatter.9.cloned.1.call-done = f32[384,24]{0,1:T(8,128)} async-done(((f32[384,1536]{0,1:T(8,128)}), f32[384,24]{0,1:T(8,128)}) %reduce-scatter.9.cloned.1.call-update) | async-done | bytes 36880
  714.6 1.4 broadcast_multiply_fusion.2
  (117 shorter events, 8.9 us)
Async XLA Ops:
  7.2 22.1 %copy-start.7 = (bf16[512,384]{1,0:T(8,128)(2,1)S(1)}, bf16[512,384]{1,0:T(8,128)(2,1)}, u32[]{:S(2)}) copy-start(bf16[512,384]{1,0:T(8,128)(2,1)} %param.8) | copy-start | bytes 1179652
  10.9 3.2 copy-start.10
  17.1 21.6 %all-to-all-start.1 = ((s32[64,1,8]{2,1,0:T(1,128)}), s32[64,1,8]{2,1,0:T(1,128)S(1)}, u32[]{:S(2)}, u32[]{:S(2)}) async-start(s32[64,1,8]{2,1,0:T(1,128)} %bitcast.4), calls=%async_computation.1 | async-start | bytes 65536 | tf_op jit(solution)/shard_map/all_to_all | solution.py:90
  38.7 19.1 %all-to-all-start = ((bf16[64,8,384]{2,1,0:T(8,128)(2,1)}), bf16[64,8,384]{2,1,0:T(8,128)(2,1)S(1)}, u32[]{:S(2)}, u32[]{:S(2)}) async-start(bf16[64,8,384]{2,1,0:T(8,128)(2,1)} %bitcast.2), calls=%async_computation | async-start | bytes 786432 | tf_op jit(solution)/shard_map/all_to_all | solution.py:89
  43.3 42.2 %all-gather.12.cloned.1.call-start = ((), (), s32[]{:S(2)}) async-start(), calls=%async_computation.9 | async-start | bytes 1966080 | tf_op jit(solution)/shard_map/all_gather | solution.py:93
  44.7 13.1 %copy-start.12 = (s32[512,1]{0,1:T(1,128)}, s32[512,1]{0,1:T(1,128)S(1)}, u32[]{:S(2)}) copy-start(s32[512,1]{0,1:T(1,128)S(1)} %compare_select_fusion) | copy-start | bytes 6148
  57.9 4.9 copy-start.14
  57.9 5.0 copy-start.15
  60.5 106.8 %all-gather.6.cloned.1.call-start = ((), (), s32[]{:S(2)}) async-start(), calls=%async_computation.5 | async-start | bytes 2396160 | tf_op jit(solution)/shard_map/all_gather | solution.py:101
  61.3 183.1 %all-gather.8.cloned.1.call-start = ((), (), s32[]{:S(2)}) async-start(), calls=%async_computation.6 | async-start | bytes 1198080 | tf_op jit(solution)/shard_map/all_gather | solution.py:102
  62.0 209.6 %all-gather.10.cloned.1.call-start = ((), (), s32[]{:S(2)}) async-start(), calls=%async_computation.7 | async-start | bytes 1966080 | tf_op jit(solution)/shard_map/all_gather | solution.py:117
  62.6 278.7 %all-reduce.21.cloned.1.call-start = ((), (), s32[]{:S(2)}) async-start(), calls=%async_computation.8 | async-start | bytes 3145728 | tf_op jit(solution)/shard_map/psum | solution.py:149
  63.0 208.7 %copy-start.25 = (f32[512]{0:T(512)}, f32[512]{0:T(512)S(1)}, u32[]{:S(2)}) copy-start(f32[512]{0:T(512)S(1)} %compare_convert_fusion) | copy-start | bytes 6148
  85.6 1.9 copy-start
  167.3 2.2 copy-start.9
  169.5 1.5 copy-start.4
  171.2 0.9 copy-start.3
  281.0 1.8 copy-start.5
  281.3 0.7 copy-start.8
  285.5 329.6 %all-reduce.23.cloned.1.call-start = ((), (), s32[]{:S(2)}) async-start(), calls=%async_computation.11 | async-start | bytes 9437184
  298.4 0.7 copy-start.26
  298.4 318.1 %reduce-scatter.7.cloned.1.call-start = ((), (), s32[]{:S(2)}) async-start(), calls=%async_computation.10 | async-start | bytes 1966080
  303.3 411.3 %reduce-scatter.9.cloned.1.call-start = ((), (), s32[]{:S(2)}) async-start(), calls=%async_computation.12 | async-start | bytes 2396160
  307.7 0.7 copy-start.13
  341.3 1.9 copy-start.1
  343.2 1.1 copy-start.6
  344.7 13.2 %copy-start.27 = (u32[256]{0:T(256)S(1)}, u32[256]{0:T(256)}, u32[]{:S(2)}) copy-start(u32[256]{0:T(256)} %constant.110) | copy-start | bytes 3076
  344.7 14.4 %copy-start.11 = (s32[512]{0:T(512)S(1)}, s32[512]{0:T(512)}, u32[]{:S(2)}) copy-start(s32[512]{0:T(512)} %copy-done.10) | copy-start | bytes 6148
  344.7 14.4 %copy-start.24 = (f32[384]{0:T(512)S(1)}, f32[384]{0:T(512)}, u32[]{:S(2)}) copy-start(f32[384]{0:T(512)} %get-tuple-element.9) | copy-start | bytes 4612
  344.8 14.4 %copy-start.23 = (f32[384]{0:T(512)S(1)}, f32[384]{0:T(512)}, u32[]{:S(2)}) copy-start(f32[384]{0:T(512)} %get-tuple-element.10) | copy-start | bytes 4612
  344.8 14.4 %copy-start.22 = (f32[384]{0:T(512)S(1)}, f32[384]{0:T(512)}, u32[]{:S(2)}) copy-start(f32[384]{0:T(512)} %get-tuple-element.11) | copy-start | bytes 4612
  344.8 14.5 %copy-start.21 = (f32[384]{0:T(512)S(1)}, f32[384]{0:T(512)}, u32[]{:S(2)}) copy-start(f32[384]{0:T(512)} %get-tuple-element.12) | copy-start | bytes 4612
  344.8 14.5 %copy-start.20 = (f32[384]{0:T(512)S(1)}, f32[384]{0:T(512)}, u32[]{:S(2)}) copy-start(f32[384]{0:T(512)} %get-tuple-element.16) | copy-start | bytes 4612
  344.8 14.5 %copy-start.19 = (f32[384]{0:T(512)S(1)}, f32[384]{0:T(512)}, u32[]{:S(2)}) copy-start(f32[384]{0:T(512)} %get-tuple-element.13) | copy-start | bytes 4612
  344.8 14.5 %copy-start.18 = (f32[384]{0:T(512)S(1)}, f32[384]{0:T(512)}, u32[]{:S(2)}) copy-start(f32[384]{0:T(512)} %get-tuple-element.14) | copy-start | bytes 4612
  344.8 14.5 %copy-start.17 = (f32[384]{0:T(512)S(1)}, f32[384]{0:T(512)}, u32[]{:S(2)}) copy-start(f32[384]{0:T(512)} %get-tuple-element.15) | copy-start | bytes 4612
  344.8 14.5 %copy-start.16 = (f32[384]{0:T(512)S(1)}, f32[384]{0:T(512)}, u32[]{:S(2)}) copy-start(f32[384]{0:T(512)} %get-tuple-element.8) | copy-start | bytes 4612
  347.4 265.0 %all-to-all-start.2 = ((bf16[64,8,384]{2,1,0:T(8,128)(2,1)}), bf16[64,8,384]{2,1,0:T(8,128)(2,1)S(1)}, u32[]{:S(2)}, u32[]{:S(2)}) async-start(bf16[64,8,384]{2,1,0:T(8,128)(2,1)} %bitcast.7), calls=%async_computation.2 | async-start | bytes 786432 | tf_op jit(solution)/shard_map/all_to_all | solution.py:161
  612.4 5.4 copy-start.2
Sparse Core Ops, SparseCore 0:
  60.6 24.8 all-gather.11
  88.2 79.0 all-gather.5
  170.0 74.3 all-gather.7
  246.1 25.4 all-gather.9
  285.6 55.6 all-reduce.20
  344.7 201.8 all-reduce.22
  549.1 25.4 reduce-scatter.6
  578.7 135.7 reduce-scatter.8
where the time goes:
time: 724 us; the launch traced here: 723 us
  waiting for transfers between devices  348 us (48%)
  blocking collectives  252 us (35%)
  local copies, waits for them, and re-layouts  36.2 us (5%)
  starting transfers between devices  27.9 us (4%)
  matrix products  23.5 us (3%)
  other arithmetic  20.3 us (3%)
  between operations  15.4 us (2%)
    psum x1, blocking collectives, shards(): gain_sum, kernel_sum = lax.psum((gain_term, kernel_term), 'dp')  252 us
    unnamed x11, waiting for transfers between devices  97.9 us
    all_gather x1, waiting for transfers between devices, shards(): lax.all_gather(expand, 'dp', axis=0, tiled=True).reshape(D, 2 * quarter)  79.3 us
    all_gather x1, waiting for transfers between devices, shards(): project_full = lax.all_gather(project, 'dp', axis=1, tiled=True)  70.2 us
    psum x1, waiting for transfers between devices, shards(): lax.psum(scaled_part.astype(jnp.bfloat16), 'seq').astype(jnp.float32)  32.9 us
    all_gather x1, waiting for transfers between devices, shards(): cot_full = lax.all_gather(cotangent, 'seq', axis=1, tiled=True)  27.2 us
    all_gather x1, waiting for transfers between devices, shards(): whole_rows = lax.all_gather(local_rows, 'seq', axis=1, tiled=True)  22.6 us
  transfers between devices with their start and end apart: 11, of which 8 were waited for; matrix products, arithmetic and copies ran while one was open for 7% of the time, Pallas kernels for 0%

commit v1 on v0

--- a/solution.py
+++ b/solution.py
@@ -60,6 +60,44 @@
     )
     padded = jnp.concatenate([flat, jnp.zeros((1, flat.shape[1]), flat.dtype)])
     return (padded[inverse], inverse < total_slots)
+
+
+def dp_bits(groups):
+    return groups.bit_length() - 1
+
+
+def halving_sum(blocks, groups):
+    me = lax.axis_index("dp")
+    bits = dp_bits(groups)
+    rest = blocks.shape[1:]
+    cur = blocks.reshape((2,) * bits + rest)
+    axis_bits = [bits - 1 - a for a in range(bits)]
+    for bit in range(bits):
+        at = axis_bits.index(bit)
+        mine = (me >> bit) & 1
+        keep = lax.dynamic_index_in_dim(cur, mine, axis=at, keepdims=False)
+        send = lax.dynamic_index_in_dim(cur, 1 - mine, axis=at, keepdims=False)
+        pairs = [(i, i ^ (1 << bit)) for i in range(groups)]
+        cur = keep + lax.ppermute(send, "dp", pairs)
+        axis_bits.pop(at)
+    return cur.reshape(rest)
+
+
+def doubling_gather(shard, groups):
+    me = lax.axis_index("dp")
+    bits = dp_bits(groups)
+    cur = shard[None]
+    held = []
+    for bit in reversed(range(bits)):
+        pairs = [(i, i ^ (1 << bit)) for i in range(groups)]
+        got = lax.ppermute(cur, "dp", pairs)
+        low = (me >> bit) & 1 == 0
+        cur = jnp.concatenate([jnp.where(low, cur, got), jnp.where(low, got, cur)], axis=0)
+        held.insert(0, bit)
+    cur = cur.reshape((2,) * bits + shard.shape)
+    order = [held.index(b) for b in reversed(range(bits))]
+    cur = jnp.transpose(cur, order + list(range(bits, bits + shard.ndim)))
+    return cur.reshape((groups * shard.shape[0],) + shard.shape[1:])
 
 
 def shards(frames, owner_slot, segment, norm_gain, expand, kernel, project, cotangent):
@@ -98,8 +136,8 @@
     inv_scale = lax.rsqrt(jnp.mean(centred * centred, axis=1, keepdims=True) + EPS)
     normed = centred * inv_scale
     scaled = (normed * norm_gain).astype(jnp.bfloat16)
-    expand_full = lax.all_gather(expand, "dp", axis=0, tiled=True).reshape(D, 2 * quarter)
-    project_full = lax.all_gather(project, "dp", axis=1, tiled=True)
+    expand_full = doubling_gather(expand, groups).reshape(D, 2 * quarter)
+    project_full = doubling_gather(project.T, groups).T
     joined = jnp.dot(scaled, expand_full, preferred_element_type=jnp.float32)
     value_half = joined[:, :quarter]
     gate_sig = jax.nn.sigmoid(joined[:, quarter:])
@@ -116,9 +154,11 @@
     inv_root = 1.0 / math.sqrt(row_count * groups)
     cot_full = lax.all_gather(cotangent, "seq", axis=1, tiled=True)
     project_term = lax.dot_general(
-        hidden, cot_full, (((0,), (0,)), ((), ())), preferred_element_type=jnp.float32
-    )
-    grad_project = lax.psum_scatter(project_term, "dp", scatter_dimension=1, tiled=True) * inv_root
+        cot_full, hidden, (((0,), (0,)), ((), ())), preferred_element_type=jnp.float32
+    )
+    grad_project = (
+        halving_sum(project_term.reshape(groups, D // groups, quarter), groups).T * inv_root
+    )
     hidden_grad = (
         lax.dot_general(
             cot_full, project_full, (((1,), (1,)), ((), ())), preferred_element_type=jnp.float32
@@ -134,13 +174,7 @@
         scaled, proj_grad, (((0,), (0,)), ((), ())), preferred_element_type=jnp.float32
     )
     grad_expand = (
-        lax.psum_scatter(
-            term_block.reshape(expand.shape[0] * lax.axis_size("dp"), 2, quarter),
-            "dp",
-            scatter_dimension=0,
-            tiled=True,
-        )
-        * inv_root
+        halving_sum(term_block.reshape(groups, expand.shape[0], 2, quarter), groups) * inv_root
     )
     scaled_part = lax.dot_general(
         proj_grad, expand_full, (((1,), (1,)), ((), ())), preferred_element_type=jnp.float32

time: 724 us -> 591 us (0.82); the launches traced: 723 us -> 579 us
  waiting for transfers between devices: 348 us -> 122 us
  starting transfers between devices: 27.9 us -> 55.6 us
  local copies, waits for them, and re-layouts: 36.2 us -> 58.8 us
  other arithmetic: 20.3 us -> 42.2 us
  blocking collectives: 252 us -> 264 us
    all_gather x2 -> x0, waiting for transfers between devices: 150 us -> none  [the longest x1 79.3 us: shards(): lax.all_gather(expand, 'dp', axis=0, tiled=True).reshape(D, 2 * quarter)]
    unnamed x11 -> x5, waiting for transfers between devices: 97.9 us -> 0.07 us
    ppermute x0 -> x24, waiting for transfers between devices: none -> 90.8 us  [the longest x12 59.2 us: halving_sum(): cur = keep + lax.ppermute(send, 'dp', pairs)]
    ppermute x0 -> x24, starting transfers between devices: none -> 28 us  [the longest x12 21.4 us: doubling_gather(): got = lax.ppermute(cur, 'dp', pairs)]
    all_gather x1, waiting for transfers between devices: 22.6 us -> 0.01 us  [shards(): whole_rows = lax.all_gather(local_rows, 'seq', axis=1, tiled=True)]
    all_gather x1, waiting for transfers between devices: 27.2 us -> 9.28 us  [shards(): cot_full = lax.all_gather(cotangent, 'seq', axis=1, tiled=True)]
    psum x1, waiting for transfers between devices: 32.9 us -> 18.4 us  [shards(): lax.psum(scaled_part.astype(jnp.bfloat16), 'seq').astype(jnp.float32)]
    psum x1, blocking collectives: 252 us -> 264 us  [shards(): gain_sum, kernel_sum = lax.psum((gain_term, kernel_term), 'dp')]
  transfers between devices with their start and end apart: 11 -> 31, of which waited for: 8 -> 13; matrix products, arithmetic and copies ran while one was open for 7% -> 16% of each run, Pallas kernels for 0% -> 0%
where the time goes in v1:
time: 591 us; the launch traced here: 579 us
  blocking collectives  264 us (45%)
  waiting for transfers between devices  122 us (21%)
  local copies, waits for them, and re-layouts  58.8 us (10%)
  starting transfers between devices  55.6 us (9%)
  other arithmetic  42.2 us (7%)
  matrix products  22.2 us (4%)
  between operations  15.3 us (3%)
    psum x1, blocking collectives, shards(): gain_sum, kernel_sum = lax.psum((gain_term, kernel_term), 'dp')  264 us
    ppermute x12, waiting for transfers between devices, halving_sum(): cur = keep + lax.ppermute(send, 'dp', pairs)  59.2 us
    ppermute x12, waiting for transfers between devices, doubling_gather(): got = lax.ppermute(cur, 'dp', pairs)  31.7 us
    ppermute x12, starting transfers between devices, doubling_gather(): got = lax.ppermute(cur, 'dp', pairs)  21.4 us
    psum x1, waiting for transfers between devices, shards(): lax.psum(scaled_part.astype(jnp.bfloat16), 'seq').astype(jnp.float32)  18.4 us
    unnamed x107, local copies, waits for them, and re-layouts  13.5 us
    all_to_all x1, starting transfers between devices, shards(): lax.all_to_all(landing_out, 'dp', split_axis=0, concat_axis=0, tiled=True)  12.1 us
  transfers between devices with their start and end apart: 31, of which 13 were waited for; matrix products, arithmetic and copies ran while one was open for 16% of the time, Pallas kernels for 0%

profile of v1, /device:TPU:4, one launch (start us, length us, event | category | flops | bytes accessed | tf_op | source)
XLA Modules:
  0.0 579.4 jit_solution(12474805233300600221)
XLA Ops:
  11.0 2.4 scatter_custom_fusion
  14.1 2.3 gather_fusion.1
  17.2 12.1 %all-to-all-start.1 = ((s32[64,1,8]{2,1,0:T(1,128)}), s32[64,1,8]{2,1,0:T(1,128)S(1)}, u32[]{:S(2)}, u32[]{:S(2)}) async-start(s32[64,1,8]{2,1,0:T(1,128)} %bitcast.4), calls=%async_computation.1 | async-start | bytes 65536 | tf_op jit(solution)/shard_map/all_to_all | solution.py:128
  29.3 3.3 collective-permute-start.6
  33.0 2.6 gather_fusion
  35.5 3.2 all-to-all-done.1
  38.7 7.1 %all-to-all-start = ((bf16[64,8,384]{2,1,0:T(8,128)(2,1)}), bf16[64,8,384]{2,1,0:T(8,128)(2,1)S(1)}, u32[]{:S(2)}, u32[]{:S(2)}) async-start(bf16[64,8,384]{2,1,0:T(8,128)(2,1)} %bitcast.2), calls=%async_computation | async-start | bytes 786432 | tf_op jit(solution)/shard_map/all_to_all | solution.py:127
  47.3 2.4 scatter_custom_fusion.1
  52.7 4.0 collective-permute-done.1
  57.1 5.7 collective-permute-start.2
  63.3 6.1 %collective-permute-done.2 = bf16[4,24,2,384]{3,2,1,0:T(2,128)(2,1)S(1)} collective-permute-done((bf16[4,24,2,384]{3,2,1,0:T(2,128)(2,1)S(1)}, bf16[4,24,2,384]{3,2,1,0:T(2,128)(2,1)S(1)}, u32[]{:S(2)}, u32[]{:S(2)}) %collective-permute-start.2) | collective-permute-done | bytes 147488 | tf_op jit(solution)/shard_map/ppermute | solution.py:93
  69.8 2.6 gather_fusion.2
  72.8 3.0 collective-permute-start.3
  75.9 9.2 %collective-permute-done.3 = bf16[8,24,2,384]{3,2,1,0:T(2,128)(2,1)S(1)} collective-permute-done((bf16[8,24,2,384]{3,2,1,0:T(2,128)(2,1)S(1)}, bf16[8,24,2,384]{3,2,1,0:T(2,128)(2,1)S(1)}, u32[]{:S(2)}, u32[]{:S(2)}) %collective-permute-start.3) | collective-permute-done | bytes 294944 | tf_op jit(solution)/shard_map/ppermute | solution.py:93
  86.6 3.0 collective-permute-start.9
  89.6 11.2 %collective-permute-done.9 = bf16[8,24,384]{2,1,0:T(8,128)(2,1)S(1)} collective-permute-done((bf16[8,24,384]{2,1,0:T(8,128)(2,1)S(1)}, bf16[8,24,384]{2,1,0:T(8,128)(2,1)S(1)}, u32[]{:S(2)}, u32[]{:S(2)}) %collective-permute-start.9) | collective-permute-done | bytes 147488 | tf_op jit(solution)/shard_map/ppermute | solution.py:93
  100.9 3.4 collective-permute-start.10
  105.6 2.6 pad_maximum_fusion.1
  116.9 2.6 broadcast_select_fusion.1
  119.5 3.0 pad_maximum_fusion
  122.6 2.2 copy.42
  124.7 1.9 copy.57
  126.6 1.8 convert_reduce_fusion
  129.7 3.2 fusion.15
  134.3 2.2 multiply_add_fusion
  136.5 9.3 %all-gather.4.cloned.1.call-done = bf16[512,1536]{1,0:T(8,128)(2,1)} async-done(((bf16[512,384]{1,0:T(8,128)(2,1)}), bf16[512,1536]{1,0:T(8,128)(2,1)}) %all-gather.4.cloned.1.call-update) | async-done | bytes 1572880 | tf_op jit(solution)/shard_map/all_gather | solution.py:155
  145.8 7.7 %multiply_reduce_fusion.1 = (f32[384]{0:T(512)}, f32[384]{0:T(512)}, f32[384]{0:T(512)}, f32[384]{0:T(512)}, f32[384]{0:T(512)}, /*index=5*/f32[384]{0:T(512)}, ...) fusion(f32[512,384]{1,0:T(8,128)} %copy-done.4, ...), kind=kOutput, calls=%fused_computation.52 | convolution fusion | flops 611054208 | bytes 5932032 | tf_op jit(solution)/shard_map/dot_general | solution.py:163
  156.8 2.6 convolution_convert_fusion
  160.4 3.7 fusion.14
  164.1 6.7 %reshape_reshape.10 = f32[2,2,2,2,2,2,24,2,384]{8,7,6,5,4,3,2,1,0:T(2,128)} reshape(f32[1536,768]{1,0:T(8,128)} %fusion.14) | data formatting | bytes 9437184 | tf_op jit(solution)/shard_map/reshape;reshape | solution.py:73
  170.8 5.7 constant_dynamic-slice_fusion.3
  179.1 2.3 convolution_bitcast_fusion
  181.4 3.1 copy.47
  184.5 2.4 dynamic-slice_bitcast_fusion
  187.2 2.6 convolution_convert_fusion.1
  191.7 1.8 bitcast_add_fusion
  196.8 18.4 %all-reduce.18.cloned.1.call-done = bf16[512,1536]{1,0:T(8,128)(2,1)} async-done(((bf16[512,1536]{1,0:T(8,128)(2,1)}), bf16[512,1536]{1,0:T(8,128)(2,1)}) %all-reduce.18.cloned.1.call-update) | async-done | bytes 1572880 | tf_op jit(solution)/shard_map/psum | solution.py:183
  215.2 2.6 fusion.13
  217.7 2.0 fusion.3
  225.6 2.5 collective-permute-start.20
  228.6 2.6 gather_fusion.3
  231.2 7.8 %all-to-all-start.2 = ((bf16[64,8,384]{2,1,0:T(8,128)(2,1)}), bf16[64,8,384]{2,1,0:T(8,128)(2,1)S(1)}, u32[]{:S(2)}, u32[]{:S(2)}) async-start(bf16[64,8,384]{2,1,0:T(8,128)(2,1)} %bitcast.128), calls=%async_computation.2 | async-start | bytes 786432 | tf_op jit(solution)/shard_map/all_to_all | solution.py:195
  239.0 263.5 %all-reduce.15 = (f32[384]{0:T(512)S(1)}, f32[9,384]{1,0:T(8,128)S(1)}) all-reduce(f32[384]{0:T(512)S(1)} %get-tuple-element.44, f32[9,384]{1,0:T(8,128)S(1)} %stack.39), channel_id=1, replica_groups=mesh['dp'=64,'seq'=4] {'dp'}, use_global_device_ids=true, to_apply=%region_12.13 | all-reduce | flops 3840 | bytes 30720 | tf_op jit(solution)/shard_map/psum | solution.py:191
  506.4 13.1 %collective-permute-done.21 = f32[2,2,24,384]{3,2,1,0:T(8,128)S(1)} collective-permute-done((f32[2,2,24,384]{3,2,1,0:T(8,128)S(1)}, f32[2,2,24,384]{3,2,1,0:T(8,128)S(1)}, u32[]{:S(2)}, u32[]{:S(2)}) %collective-permute-start.21) | collective-permute-done | bytes 147488 | tf_op jit(solution)/shard_map/ppermute | solution.py:81
  519.7 24.2 %collective-permute-done.14 = f32[2,2,2,24,2,384]{5,3,4,2,1,0:T(8,128)S(1)} collective-permute-done((f32[2,2,2,24,2,384]{5,3,4,2,1,0:T(8,128)S(1)}, f32[2,2,2,24,2,384]{5,3,4,2,1,0:T(8,128)S(1)}, u32[]{:S(2)}, u32[]{:S(2)}) %collective-permute-start.14) | collective-permute-done | bytes 589856 | tf_op jit(solution)/shard_map/ppermute | solution.py:81
  544.2 16.2 %collective-permute-done.15 = f32[2,2,24,2,384]{4,2,3,1,0:T(8,128)S(1)} collective-permute-done((f32[2,2,24,2,384]{4,2,3,1,0:T(8,128)S(1)}, f32[2,2,24,2,384]{4,2,3,1,0:T(8,128)S(1)}, u32[]{:S(2)}, u32[]{:S(2)}) %collective-permute-start.15) | collective-permute-done | bytes 294944 | tf_op jit(solution)/shard_map/ppermute | solution.py:81
  561.3 2.6 gather_fusion.4
  566.8 5.0 collective-permute-done.17
  (250 shorter events, 52.4 us)
Async XLA Ops:
  7.2 22.1 %copy-start.27 = (bf16[384,24]{0,1:T(8,128)(2,1)S(1)}, bf16[384,24]{0,1:T(8,128)(2,1)}, u32[]{:S(2)}) copy-start(bf16[384,24]{0,1:T(8,128)(2,1)} %param.14) | copy-start | bytes 55300
  7.2 25.4 %copy-start.13 = (bf16[24,2,384]{2,1,0:T(2,128)(2,1)S(1)}, bf16[24,2,384]{2,1,0:T(2,128)(2,1)}, u32[]{:S(2)}) copy-start(bf16[24,2,384]{2,1,0:T(2,128)(2,1)} %param.12) | copy-start | bytes 110596
  7.2 25.7 %copy-start.10 = (bf16[512,384]{1,0:T(8,128)(2,1)S(1)}, bf16[512,384]{1,0:T(8,128)(2,1)}, u32[]{:S(2)}) copy-start(bf16[512,384]{1,0:T(8,128)(2,1)} %param.8) | copy-start | bytes 1179652
  11.0 21.6 %copy-start.35 = (s32[512]{0:T(512)}, s32[512]{0:T(512)S(1)}, u32[]{:S(2)}) copy-start(s32[512]{0:T(512)S(1)} %compare_select_fusion.3) | copy-start | bytes 6148
  17.2 21.6 %all-to-all-start.1 = ((s32[64,1,8]{2,1,0:T(1,128)}), s32[64,1,8]{2,1,0:T(1,128)S(1)}, u32[]{:S(2)}, u32[]{:S(2)}) async-start(s32[64,1,8]{2,1,0:T(1,128)} %bitcast.4), calls=%async_computation.1 | async-start | bytes 65536 | tf_op jit(solution)/shard_map/all_to_all | solution.py:128
  29.3 21.0 %collective-permute-start.6 = (bf16[1,24,384]{2,1,0:T(8,128)(2,1)S(1)}, bf16[1,24,384]{2,1,0:T(8,128)(2,1)S(1)}, u32[]{:S(2)}, u32[]{:S(2)}) collective-permute-start(bf16[1,24,384]{2,1,0:T(8,128)(2,1)S(1)} %bitcast.135), channel_id=1, source_target_pairs={{0,128},{4,132},{8,136},{12,140},{16,144},{20,148},{24,152},{28,15... | collective-permute-start | bytes 55304 | tf_op jit(solution)/shard_map/ppermute | solution.py:93
  32.5 17.8 %collective-permute-start = (bf16[1,24,2,384]{3,2,1,0:T(2,128)(2,1)S(1)}, bf16[1,24,2,384]{3,2,1,0:T(2,128)(2,1)S(1)}, u32[]{:S(2)}, u32[]{:S(2)}) collective-permute-start(bf16[1,24,2,384]{3,2,1,0:T(2,128)(2,1)S(1)} %bitcast.134), channel_id=1, source_target_pairs={{0,128},{4,132},{8,136},{12,140},{16,144},{20,148},{24,152},{28,15... | collective-permute-start | bytes 110600 | tf_op jit(solution)/shard_map/ppermute | solution.py:93
  38.7 31.0 %all-to-all-start = ((bf16[64,8,384]{2,1,0:T(8,128)(2,1)}), bf16[64,8,384]{2,1,0:T(8,128)(2,1)S(1)}, u32[]{:S(2)}, u32[]{:S(2)}) async-start(bf16[64,8,384]{2,1,0:T(8,128)(2,1)} %bitcast.2), calls=%async_computation | async-start | bytes 786432 | tf_op jit(solution)/shard_map/all_to_all | solution.py:127
  45.9 80.8 %all-gather.6.cloned.1.call-start = ((), (), s32[]{:S(2)}) async-start(), calls=%async_computation.6 | async-start | bytes 1966080 | tf_op jit(solution)/shard_map/all_gather | solution.py:131
  47.3 2.5 copy-start.37
  50.5 6.2 %collective-permute-start.1 = (bf16[2,24,2,384]{3,2,1,0:T(2,128)(2,1)S(1)}, bf16[2,24,2,384]{3,2,1,0:T(2,128)(2,1)S(1)}, u32[]{:S(2)}, u32[]{:S(2)}) collective-permute-start(bf16[2,24,2,384]{3,2,1,0:T(2,128)(2,1)S(1)} %pad_maximum_fusion.12), channel_id=1, source_target_pairs={{0,64},{4,68},{8,72},{12,76},{16,80},{20,84},{24,88},{28,92},{32,9... | collective-permute-start | bytes 221192 | tf_op jit(solution)/shard_map/ppermute | solution.py:93
  52.2 10.7 %collective-permute-start.7 = (bf16[2,24,384]{2,1,0:T(8,128)(2,1)S(1)}, bf16[2,24,384]{2,1,0:T(8,128)(2,1)S(1)}, u32[]{:S(2)}, u32[]{:S(2)}) collective-permute-start(bf16[2,24,384]{2,1,0:T(8,128)(2,1)S(1)} %pad_maximum_fusion.14), channel_id=1, source_target_pairs={{0,64},{4,68},{8,72},{12,76},{16,80},{20,84},{24,88},{28,92},{32,9... | collective-permute-start | bytes 110600 | tf_op jit(solution)/shard_map/ppermute | solution.py:93
  57.1 12.3 %collective-permute-start.2 = (bf16[4,24,2,384]{3,2,1,0:T(2,128)(2,1)S(1)}, bf16[4,24,2,384]{3,2,1,0:T(2,128)(2,1)S(1)}, u32[]{:S(2)}, u32[]{:S(2)}) collective-permute-start(bf16[4,24,2,384]{3,2,1,0:T(2,128)(2,1)S(1)} %pad_maximum_fusion.10), channel_id=1, source_target_pairs={{0,32},{4,36},{8,40},{12,44},{16,48},{20,52},{24,56},{28,60},{32,0... | collective-permute-start | bytes 442376 | tf_op jit(solution)/shard_map/ppermute | solution.py:93
  62.9 12.9 %collective-permute-start.8 = (bf16[4,24,384]{2,1,0:T(8,128)(2,1)S(1)}, bf16[4,24,384]{2,1,0:T(8,128)(2,1)S(1)}, u32[]{:S(2)}, u32[]{:S(2)}) collective-permute-start(bf16[4,24,384]{2,1,0:T(8,128)(2,1)S(1)} %pad_maximum_fusion.13), channel_id=1, source_target_pairs={{0,32},{4,36},{8,40},{12,44},{16,48},{20,52},{24,56},{28,60},{32,0... | collective-permute-start | bytes 221192 | tf_op jit(solution)/shard_map/ppermute | solution.py:93
  72.4 73.4 %all-gather.4.cloned.1.call-start = ((), (), s32[]{:S(2)}) async-start(), calls=%async_computation.4 | async-start | bytes 1966080 | tf_op jit(solution)/shard_map/all_gather | solution.py:155
  72.8 12.2 %collective-permute-start.3 = (bf16[8,24,2,384]{3,2,1,0:T(2,128)(2,1)S(1)}, bf16[8,24,2,384]{3,2,1,0:T(2,128)(2,1)S(1)}, u32[]{:S(2)}, u32[]{:S(2)}) collective-permute-start(bf16[8,24,2,384]{3,2,1,0:T(2,128)(2,1)S(1)} %pad_maximum_fusion.8), channel_id=1, source_target_pairs={{0,16},{4,20},{8,24},{12,28},{16,0},{20,4},{24,8},{28,12},{32,48},... | collective-permute-start | bytes 884744 | tf_op jit(solution)/shard_map/ppermute | solution.py:93
  86.5 17.9 %collective-permute-start.4 = (bf16[16,24,2,384]{3,2,1,0:T(2,128)(2,1)S(1)}, bf16[16,24,2,384]{3,2,1,0:T(2,128)(2,1)S(1)}, u32[]{:S(2)}, u32[]{:S(2)}) collective-permute-start(bf16[16,24,2,384]{3,2,1,0:T(2,128)(2,1)S(1)} %pad_maximum_fusion.4), channel_id=1, source_target_pairs={{0,8},{4,12},{8,0},{12,4},{16,24},{20,28},{24,16},{28,20},{32,40},... | collective-permute-start | bytes 1769480 | tf_op jit(solution)/shard_map/ppermute | solution.py:93
  86.6 14.2 %collective-permute-start.9 = (bf16[8,24,384]{2,1,0:T(8,128)(2,1)S(1)}, bf16[8,24,384]{2,1,0:T(8,128)(2,1)S(1)}, u32[]{:S(2)}, u32[]{:S(2)}) collective-permute-start(bf16[8,24,384]{2,1,0:T(8,128)(2,1)S(1)} %pad_maximum_fusion.11), channel_id=1, source_target_pairs={{0,16},{4,20},{8,24},{12,28},{16,0},{20,4},{24,8},{28,12},{32,48},... | collective-permute-start | bytes 442376 | tf_op jit(solution)/shard_map/ppermute | solution.py:93
  100.9 8.4 %collective-permute-start.10 = (bf16[16,24,384]{2,1,0:T(8,128)(2,1)S(1)}, bf16[16,24,384]{2,1,0:T(8,128)(2,1)S(1)}, u32[]{:S(2)}, u32[]{:S(2)}) collective-permute-start(bf16[16,24,384]{2,1,0:T(8,128)(2,1)S(1)} %pad_maximum_fusion.9), channel_id=1, source_target_pairs={{0,8},{4,12},{8,0},{12,4},{16,24},{20,28},{24,16},{28,20},{32,40},... | collective-permute-start | bytes 884744 | tf_op jit(solution)/shard_map/ppermute | solution.py:93
  108.2 8.7 %collective-permute-start.5 = (bf16[32,24,2,384]{3,2,1,0:T(2,128)(2,1)}, bf16[32,24,2,384]{3,2,1,0:T(2,128)(2,1)S(1)}, u32[]{:S(2)}, u32[]{:S(2)}) collective-permute-start(bf16[32,24,2,384]{3,2,1,0:T(2,128)(2,1)} %pad_maximum_fusion.1), channel_id=1, source_target_pairs={{0,4},{4,0},{8,12},{12,8},{16,20},{20,16},{24,28},{28,24},{32,36},... | collective-permute-start | bytes 3538952 | tf_op jit(solution)/shard_map/ppermute | solution.py:93
  110.3 5.1 collective-permute-start.11
  110.3 104.8 %all-reduce.18.cloned.1.call-start = ((), (), s32[]{:S(2)}) async-start(), calls=%async_computation.5 | async-start | bytes 3145728 | tf_op jit(solution)/shard_map/psum | solution.py:183
  126.6 1.9 copy-start
  126.6 3.0 copy-start.31
  133.0 12.7 %copy-start.48 = (f32[512]{0:T(512)S(1)}, f32[512]{0:T(512)}, u32[]{:S(2)}) copy-start(f32[512]{0:T(512)} %compare_convert_fusion) | copy-start | bytes 6148
  155.0 1.8 copy-start.5
  159.4 404.5 %reduce-scatter.4.cloned.1.call-start = ((), (), s32[]{:S(2)}) async-start(), calls=%async_computation.7 | async-start | bytes 1966080
  176.6 2.5 copy-start.50
  178.3 39.4 %collective-permute-start.12 = (f32[2,2,2,2,2,24,2,384]{7,5,6,4,3,2,1,0:T(8,128)}, f32[2,2,2,2,2,24,2,384]{7,5,6,4,3,2,1,0:T(8,128)}, u32[]{:S(2)}, u32[]{:S(2)}) collective-permute-start(f32[2,2,2,2,2,24,2,384]{7,5,6,4,3,2,1,0:T(8,128)} %bitcast.118), channel_id=1, source_target_pairs={{0,4},{4,0},{8,12},{12,8},{16,20},{20,16},{24,28},{28,24},{32,36},... | collective-permute-start | bytes 7077896 | tf_op jit(solution)/shard_map/ppermute | solution.py:81
  184.5 2.6 copy-start.36
  184.5 2.7 copy-start.38
  186.9 4.8 collective-permute-start.18
  189.9 1.8 copy-start.39
  195.2 27.7 %collective-permute-start.19 = (f32[2,2,2,2,24,384]{5,4,2,1,0,3:T(8,128)}, f32[2,2,2,2,24,384]{5,4,2,1,0,3:T(8,128)S(1)}, u32[]{:S(2)}, u32[]{:S(2)}) collective-permute-start(f32[2,2,2,2,24,384]{5,4,2,1,0,3:T(8,128)} %bitcast.119), channel_id=1, source_target_pairs={{0,8},{4,12},{8,0},{12,4},{16,24},{20,28},{24,16},{28,20},{32,40},... | collective-permute-start | bytes 1769480 | tf_op jit(solution)/shard_map/ppermute | solution.py:81
  215.2 2.6 copy-start.1
  219.8 2.7 copy-start.2
  220.9 283.2 %collective-permute-start.13 = (f32[2,2,2,2,24,2,384]{6,4,5,3,2,1,0:T(8,128)}, f32[2,2,2,2,24,2,384]{6,4,5,3,2,1,0:T(8,128)}, u32[]{:S(2)}, u32[]{:S(2)}) collective-permute-start(f32[2,2,2,2,24,2,384]{6,4,5,3,2,1,0:T(8,128)} %dynamic-slice_bitcast_fusion.1), channel_id=1, source_target_pairs={{0,8},{4,12},{8,0},{12,4},{16,24},{20,28},{24,16},{28,20},{32,40},... | collective-permute-start | bytes 3538952 | tf_op jit(solution)/shard_map/ppermute | solution.py:81
  222.9 5.3 copy-start.7
  225.6 277.5 %collective-permute-start.20 = (f32[2,2,2,24,384]{4,3,2,1,0:T(8,128)}, f32[2,2,2,24,384]{4,3,2,1,0:T(8,128)}, u32[]{:S(2)}, u32[]{:S(2)}) collective-permute-start(f32[2,2,2,24,384]{4,3,2,1,0:T(8,128)} %dynamic-slice_bitcast_fusion.3), channel_id=1, source_target_pairs={{0,16},{4,20},{8,24},{12,28},{16,0},{20,4},{24,8},{28,12},{32,48},... | collective-permute-start | bytes 884744 | tf_op jit(solution)/shard_map/ppermute | solution.py:81
  231.2 330.1 %all-to-all-start.2 = ((bf16[64,8,384]{2,1,0:T(8,128)(2,1)}), bf16[64,8,384]{2,1,0:T(8,128)(2,1)S(1)}, u32[]{:S(2)}, u32[]{:S(2)}) async-start(bf16[64,8,384]{2,1,0:T(8,128)(2,1)} %bitcast.128), calls=%async_computation.2 | async-start | bytes 786432 | tf_op jit(solution)/shard_map/all_to_all | solution.py:195
  505.6 38.3 %collective-permute-start.14 = (f32[2,2,2,24,2,384]{5,3,4,2,1,0:T(8,128)S(1)}, f32[2,2,2,24,2,384]{5,3,4,2,1,0:T(8,128)S(1)}, u32[]{:S(2)}, u32[]{:S(2)}) collective-permute-start(f32[2,2,2,24,2,384]{5,3,4,2,1,0:T(8,128)S(1)} %dynamic-slice_bitcast_fusion.2), channel_id=1, source_target_pairs={{0,16},{4,20},{8,24},{12,28},{16,0},{20,4},{24,8},{28,12},{32,48},... | collective-permute-start | bytes 1769480 | tf_op jit(solution)/shard_map/ppermute | solution.py:81
  505.7 13.8 %collective-permute-start.21 = (f32[2,2,24,384]{3,2,1,0:T(8,128)S(1)}, f32[2,2,24,384]{3,2,1,0:T(8,128)S(1)}, u32[]{:S(2)}, u32[]{:S(2)}) collective-permute-start(f32[2,2,24,384]{3,2,1,0:T(8,128)S(1)} %dynamic-slice_bitcast_fusion.5), channel_id=1, source_target_pairs={{0,32},{4,36},{8,40},{12,44},{16,48},{20,52},{24,56},{28,60},{32,0... | collective-permute-start | bytes 442376 | tf_op jit(solution)/shard_map/ppermute | solution.py:81
  519.6 24.5 %collective-permute-start.22 = (f32[2,24,384]{2,1,0:T(8,128)S(1)}, f32[2,24,384]{2,1,0:T(8,128)S(1)}, u32[]{:S(2)}, u32[]{:S(2)}) collective-permute-start(f32[2,24,384]{2,1,0:T(8,128)S(1)} %dynamic-slice_bitcast_fusion.7), channel_id=1, source_target_pairs={{0,64},{4,68},{8,72},{12,76},{16,80},{20,84},{24,88},{28,92},{32,9... | collective-permute-start | bytes 221192 | tf_op jit(solution)/shard_map/ppermute | solution.py:81
  544.0 16.5 %collective-permute-start.15 = (f32[2,2,24,2,384]{4,2,3,1,0:T(8,128)S(1)}, f32[2,2,24,2,384]{4,2,3,1,0:T(8,128)S(1)}, u32[]{:S(2)}, u32[]{:S(2)}) collective-permute-start(f32[2,2,24,2,384]{4,2,3,1,0:T(8,128)S(1)} %dynamic-slice_bitcast_fusion.4), channel_id=1, source_target_pairs={{0,32},{4,36},{8,40},{12,44},{16,48},{20,52},{24,56},{28,60},{32,0... | collective-permute-start | bytes 884744 | tf_op jit(solution)/shard_map/ppermute | solution.py:81
  544.1 16.5 %collective-permute-start.23 = (f32[24,384]{1,0:T(8,128)S(1)}, f32[24,384]{1,0:T(8,128)S(1)}, u32[]{:S(2)}, u32[]{:S(2)}) collective-permute-start(f32[24,384]{1,0:T(8,128)S(1)} %dynamic-slice_bitcast_fusion.9), channel_id=1, source_target_pairs={{0,128},{4,132},{8,136},{12,140},{16,144},{20,148},{24,152},{28,15... | collective-permute-start | bytes 110600 | tf_op jit(solution)/shard_map/ppermute | solution.py:81
  560.6 5.2 collective-permute-start.16
  563.9 2.0 copy-start.3
  565.8 5.9 %collective-permute-start.17 = (f32[24,2,384]{2,0,1:T(8,128)S(1)}, f32[24,2,384]{2,0,1:T(8,128)S(1)}, u32[]{:S(2)}, u32[]{:S(2)}) collective-permute-start(f32[24,2,384]{2,0,1:T(8,128)S(1)} %dynamic-slice_bitcast_fusion.8), channel_id=1, source_target_pairs={{0,128},{4,132},{8,136},{12,140},{16,144},{20,148},{24,152},{28,15... | collective-permute-start | bytes 221192 | tf_op jit(solution)/shard_map/ppermute | solution.py:81
  (34 other events, 42.6 us)
Sparse Core Ops, SparseCore 0:
  72.5 29.9 all-gather.5
  110.5 35.2 all-gather.3
  159.5 55.5 all-reduce.17
  217.6 27.9 reduce-scatter.3
